TPU v7x, 128 devices: a whole 4x4x4 slice. The times are simulated.
128 devices in a mesh: seq: 32 (over y, z, core), head: 4 (over x).
Axes of the slice: x: 4, y: 4, z: 4, core: 2. Of those that a mesh axis runs over, the one named last changes fastest.
Arguments:
- queries: bfloat16 [8192, 2048], P('seq', 'head'), parts along dimension 1, may hold values from -6 to 6
- keys: bfloat16 [8192, 512], P('seq', 'head'), parts along dimension 1, may hold values from -6 to 6
- values: bfloat16 [8192, 512], P('seq', 'head'), parts along dimension 1, may hold values from -6 to 6
- grad_out: bfloat16 [8192, 2048], P('seq', 'head'), parts along dimension 1, may hold values from -6 to 6
- lengths: int32 [16], replicated, may hold values from 1 to 2048, 8192 in all
- send_order: int32 [32, 256], replicated, may hold values from 0 to 255, each once within a row
Outputs:
- attended: float32 [8192, 2048], P('seq', 'head'), parts along dimension 1
- grad_queries: float32 [8192, 2048], P('seq', 'head'), parts along dimension 1
- grad_keys: float32 [8192, 512], P('seq', 'head'), parts along dimension 1
- grad_values: float32 [8192, 512], P('seq', 'head'), parts along dimension 1
There are 4 independent parts, one for each index of `head`. A program takes and returns all parts, laid end to end along the dimension named above; an argument that names none is the same for every part. Nothing has to cross between parts.
Inputs may be any that keep to these rules, and one draw needn't show every extreme that they name: `lengths`: they sum to 8192; the longest is exactly 2048. `send_order`: each row is a permutation of 0 to 255.
All inputs are finite; a program needn't handle non-finite values.
Results may differ from a plain program's by a relative error of at most 0.039.
Values may be sent and summed in bfloat16 or wider, within the bound.
No kernel may reach another device: no remote copies, remote signals or barrier semaphores. Data moves between devices by JAX's collectives and lax.ppermute only.
A program may use at most 64 MiB of HBM per device.

v0:
```python
import math
import jax
import jax.numpy as jnp
from jax import lax
from jax.sharding import PartitionSpec as P

masked_value = -1e30


def doc_index(positions, bounds):
    return jnp.sum((positions[:, None] >= bounds[None, :]).astype(jnp.int32), axis=1)


def visible(query_pos, query_doc, key_pos, bounds):
    key_doc = doc_index(key_pos, bounds)
    return ((query_doc[:, None] == key_doc[None, :]) & (key_pos[None, :] <= query_pos[:, None]))[
        :, None, :
    ]


def block_scores(query_heads, key_block, allowed, score_scale):
    products = (
        jnp.einsum("bhd,td->bht", query_heads, key_block, preferred_element_type=jnp.float32)
        * score_scale
    )
    return jnp.where(allowed, products, masked_value)


def key_blocks(key_piece, value_piece):
    piece_rows = key_piece.shape[0]
    block_rows = math.gcd(piece_rows, 512)
    block_count = piece_rows // block_rows
    offsets = block_rows * jnp.arange(block_count, dtype=jnp.int32)
    stacked = (
        key_piece.reshape(block_count, block_rows, key_piece.shape[1]),
        value_piece.reshape(block_count, block_rows, value_piece.shape[1]),
        offsets,
    )
    return (stacked, block_rows)


def forward_piece(run_state, key_piece, value_piece, context):
    query_heads, query_pos, query_doc, bounds, score_scale = context
    stacked, block_rows = key_blocks(key_piece, value_piece)

    def forward_update(loop_state, block_item):
        run_max, run_total, weighted = loop_state
        key_block, value_block, offset = block_item
        allowed = visible(
            query_pos, query_doc, offset + jnp.arange(block_rows, dtype=jnp.int32), bounds
        )
        scores = block_scores(query_heads, key_block, allowed, score_scale)
        new_max = jnp.maximum(run_max, jnp.max(scores, axis=2))
        exp_weights = jnp.where(allowed, jnp.exp(scores - new_max[:, :, None]), 0.0)
        rescale = jnp.exp(run_max - new_max)
        run_total = run_total * rescale + jnp.sum(exp_weights, axis=2)
        weighted = weighted * rescale[:, :, None] + jnp.einsum(
            "bht,td->bhd",
            exp_weights.astype(jnp.bfloat16),
            value_block,
            preferred_element_type=jnp.float32,
        )
        return ((new_max, run_total, weighted), None)

    run_state, _ = lax.scan(forward_update, run_state, stacked)
    return run_state


def backward_piece(key_piece, value_piece, context):
    query_heads, grad_heads, query_pos, query_doc, bounds, score_scale, log_total, out_dot = context
    stacked, block_rows = key_blocks(key_piece, value_piece)

    def backward_update(query_sum, block_item):
        key_block, value_block, offset = block_item
        allowed = visible(
            query_pos, query_doc, offset + jnp.arange(block_rows, dtype=jnp.int32), bounds
        )
        scores = block_scores(query_heads, key_block, allowed, score_scale)
        weights = jnp.where(allowed, jnp.exp(scores - log_total[:, :, None]), 0.0)
        grad_dots = jnp.einsum(
            "bhd,td->bht", grad_heads, value_block, preferred_element_type=jnp.float32
        )
        score_grads = (weights * (grad_dots - out_dot[:, :, None])).astype(jnp.bfloat16)
        query_sum = query_sum + jnp.einsum(
            "bht,td->bhd", score_grads, key_block, preferred_element_type=jnp.float32
        )
        key_term = (
            jnp.einsum("bht,bhd->td", score_grads, query_heads, preferred_element_type=jnp.float32)
            * score_scale
        )
        value_term = jnp.einsum(
            "bht,bhd->td",
            weights.astype(jnp.bfloat16),
            grad_heads,
            preferred_element_type=jnp.float32,
        )
        return (query_sum, (key_term, value_term))

    zero_query = jnp.zeros(query_heads.shape, jnp.float32)
    query_add, (key_terms, value_terms) = lax.scan(backward_update, zero_query, stacked)
    piece_rows = key_piece.shape[0]
    return (query_add, key_terms.reshape(piece_rows, -1), value_terms.reshape(piece_rows, -1))


def per_device(queries, keys, values, grad_out, lengths, send_order):
    shard_count = lax.axis_size("seq")
    my_index = lax.axis_index("seq")
    tok_rows, head_dim = keys.shape
    group_rows = tok_rows // shard_count
    head_count = queries.shape[1] // head_dim
    score_scale = 1.0 / math.sqrt(head_dim)
    bounds = jnp.cumsum(lengths)
    own_order = lax.dynamic_index_in_dim(send_order, my_index, 0, keepdims=False)
    outgoing = jnp.take(queries, own_order, axis=0)
    picked = lax.all_to_all(outgoing, "seq", split_axis=0, concat_axis=0, tiled=True)
    columns = lax.dynamic_slice_in_dim(send_order, my_index * group_rows, group_rows, 1)
    query_pos = (jnp.arange(shard_count, dtype=jnp.int32)[:, None] * tok_rows + columns).reshape(
        tok_rows
    )
    query_doc = doc_index(query_pos, bounds)
    query_heads = picked.reshape(tok_rows, head_count, head_dim)
    grad_heads = grad_out.reshape(tok_rows, head_count, head_dim)
    context = (query_heads, query_pos, query_doc, bounds, score_scale)
    start_state = (
        jnp.full((tok_rows, head_count), masked_value, jnp.float32),
        jnp.zeros((tok_rows, head_count), jnp.float32),
        jnp.zeros((tok_rows, head_count, head_dim), jnp.float32),
    )
    piece_pair = (
        lax.all_gather(keys, "seq", axis=0, tiled=True),
        lax.all_gather(values, "seq", axis=0, tiled=True),
    )
    run_max, run_total, weighted = forward_piece(start_state, piece_pair[0], piece_pair[1], context)
    attended = weighted / run_total[:, :, None]
    attended_low = attended.astype(jnp.bfloat16)
    log_total = run_max + jnp.log(run_total)
    out_dot = jnp.sum(grad_heads.astype(jnp.float32) * attended_low.astype(jnp.float32), axis=2)
    grad_context = (
        query_heads,
        grad_heads,
        query_pos,
        query_doc,
        bounds,
        score_scale,
        log_total,
        out_dot,
    )
    piece_pair = (
        lax.all_gather(keys, "seq", axis=0, tiled=True),
        lax.all_gather(values, "seq", axis=0, tiled=True),
    )
    query_add, key_part, value_part = backward_piece(piece_pair[0], piece_pair[1], grad_context)
    key_all = key_part
    value_all = value_part
    query_sum, key_all, value_all = (query_add, key_all, value_all)
    key_grad, value_grad = (
        lax.psum_scatter(key_all, "seq", scatter_dimension=0, tiled=True),
        lax.psum_scatter(value_all, "seq", scatter_dimension=0, tiled=True),
    )
    grad_queries = (query_sum * score_scale).reshape(tok_rows, head_count * head_dim)
    return (attended.reshape(tok_rows, head_count * head_dim), grad_queries, key_grad, value_grad)


def solution(mesh):
    placed = (P("seq", "head"), P("seq", "head"), P("seq", "head"), P("seq", "head"), P(), P())
    return jax.shard_map(
        per_device,
        mesh=mesh,
        in_specs=placed,
        out_specs=(P("seq", "head"), P("seq", "head"), P("seq", "head"), P("seq", "head")),
        check_vma=False,
    )
```

profile of v0, /device:TPU:0, one launch (start us, length us, event | category | flops | bytes accessed | tf_op | source)
XLA Modules:
  0.0 495.6 jit_solution(17738057707198617605)
XLA Ops:
  12.2 8.4 %all-to-all-start = ((bf16[32,8,512]{2,1,0:T(8,128)(2,1)}), bf16[32,8,512]{2,1,0:T(8,128)(2,1)S(1)}, u32[]{:S(2)}, u32[]{:S(2)}) async-start(bf16[32,8,512]{2,1,0:T(8,128)(2,1)} %bitcast_select_fusion.2), calls=%async_computation | async-start | bytes 524288 | tf_op jit(solution)/shard_map/all_to_all | solution.py:115
  21.8 8.0 %all-to-all-done = bf16[32,8,512]{2,1,0:T(8,128)(2,1)S(1)} async-done(((bf16[32,8,512]{2,1,0:T(8,128)(2,1)}), bf16[32,8,512]{2,1,0:T(8,128)(2,1)S(1)}, u32[]{:S(2)}, u32[]{:S(2)}) %all-to-all-start) | async-done | bytes 262176 | tf_op jit(solution)/shard_map/all_to_all | solution.py:115
  29.9 26.8 %all-gather.3.cloned.1.call-done = bf16[8192,128]{1,0:T(8,128)(2,1)} async-done(((bf16[256,128]{1,0:T(8,128)(2,1)}), bf16[8192,128]{1,0:T(8,128)(2,1)}) %all-gather.3.cloned.1.call-update) | async-done | bytes 2097168 | tf_op jit(solution)/shard_map/all_gather | solution.py:130
  56.7 45.3 %all-gather.5.cloned.1.call-done = bf16[8192,128]{1,0:T(8,128)(2,1)} async-done(((bf16[256,128]{1,0:T(8,128)(2,1)}), bf16[8192,128]{1,0:T(8,128)(2,1)}) %all-gather.5.cloned.1.call-update) | async-done | bytes 2097168 | tf_op jit(solution)/shard_map/all_gather | solution.py:131
  102.0 85.3 %while.32 = (s32[]{:T(128)}, f32[256,4]{0,1:T(4,128)S(1)}, f32[256,4]{0,1:T(4,128)S(1)}, f32[256,4,128]{2,0,1:T(8,128)S(1)}, s32[256]{0:T(256)S(1)}, /*index=5*/...) while((s32[]{:T(128)}, f32[256,4]{0,1:T(4,128)S(1)}, ...), condition=%wide.wide.region_6.7_spmd.clone, body=%wide.wide.region_2.6_spmd.clone.sunk | while | flops 276067328 | bytes 8466673 | solution.py:65
  105.5 1.8 convolution_add_fusion.6
  108.9 1.4 fusion.88
  110.8 1.8 convolution_add_fusion.6
  114.2 1.4 fusion.88
  116.2 1.8 convolution_add_fusion.6
  121.5 1.8 convolution_add_fusion.6
  124.9 1.4 fusion.88
  126.8 1.8 convolution_add_fusion.6
  130.2 1.4 fusion.88
  132.1 1.8 convolution_add_fusion.6
  137.5 1.8 convolution_add_fusion.6
  140.8 1.4 fusion.88
  142.8 1.8 convolution_add_fusion.6
  146.2 1.4 fusion.88
  148.1 1.8 convolution_add_fusion.6
  153.5 1.8 convolution_add_fusion.6
  156.8 1.4 fusion.88
  158.8 1.8 convolution_add_fusion.6
  162.2 1.4 fusion.88
  164.1 1.8 convolution_add_fusion.6
  169.5 1.8 convolution_add_fusion.6
  174.8 1.8 convolution_add_fusion.6
  180.1 1.8 convolution_add_fusion.6
  185.5 1.8 convolution_add_fusion.6
  187.6 133.8 %while.33 = (s32[]{:T(128)}, f32[256,4,128]{2,0,1:T(8,128)S(1)}, f32[16,512,128]{2,1,0:T(8,128)}, f32[16,512,128]{2,1,0:T(8,128)}, s32[256]{0:T(256)S(1)}, /*ind...) while((s32[]{:T(128)}, f32[256,4,128]{2,0,1:T(8,128)S(1)}, ...), condition=%wide.wide.region_10.11_spmd.clone, body=%wide.wide.region_8.10_spmd.clone.sunk | while | flops 676028416 | bytes 12734739 | solution.py:100
  189.1 1.6 fusion.101
  192.1 1.6 convolution_add_fusion.7
  197.5 1.6 fusion.101
  200.4 1.6 convolution_add_fusion.7
  205.8 1.6 fusion.101
  208.8 1.6 convolution_add_fusion.7
  214.2 1.6 fusion.101
  217.1 1.6 convolution_add_fusion.7
  222.6 1.6 fusion.101
  225.5 1.6 convolution_add_fusion.7
  230.9 1.6 fusion.101
  233.9 1.6 convolution_add_fusion.7
  239.3 1.6 fusion.101
  242.3 1.6 convolution_add_fusion.7
  247.7 1.6 fusion.101
  250.6 1.6 convolution_add_fusion.7
  256.0 1.6 fusion.101
  259.0 1.6 convolution_add_fusion.7
  264.4 1.6 fusion.101
  267.4 1.6 convolution_add_fusion.7
  272.8 1.6 fusion.101
  275.7 1.6 convolution_add_fusion.7
  281.1 1.6 fusion.101
  284.1 1.6 convolution_add_fusion.7
  289.5 1.6 fusion.101
  292.5 1.6 convolution_add_fusion.7
  297.9 1.6 fusion.101
  300.8 1.6 convolution_add_fusion.7
  306.2 1.6 fusion.101
  309.2 1.6 convolution_add_fusion.7
  314.6 1.6 fusion.101
  317.5 1.6 convolution_add_fusion.7
  323.9 79.4 %reduce-scatter.5.cloned.1.call-done = f32[256,128]{1,0:T(8,128)} async-done(((f32[8192,128]{1,0:T(8,128)}), f32[256,128]{1,0:T(8,128)}) %reduce-scatter.5.cloned.1.call-update) | async-done | bytes 131088 | tf_op jit(solution)/shard_map/reduce_scatter | solution.py:158
  403.3 85.8 %reduce-scatter.3.cloned.1.call-done = f32[256,128]{1,0:T(8,128)} async-done(((f32[8192,128]{1,0:T(8,128)}), f32[256,128]{1,0:T(8,128)}) %reduce-scatter.3.cloned.1.call-update) | async-done | bytes 131088 | tf_op jit(solution)/shard_map/reduce_scatter | solution.py:157
  (298 shorter events, 136.0 us)
Async XLA Ops:
  7.2 3.1 copy-start
  7.2 13.5 %copy-start.3 = (s32[32,256]{1,0:T(8,128)S(1)}, s32[32,256]{1,0:T(8,128)}, u32[]{:S(2)}) copy-start(s32[32,256]{1,0:T(8,128)} %param.15) | copy-start | bytes 98308
  7.2 13.9 %copy-start.4 = (s32[16]{0:T(128)S(1)}, s32[16]{0:T(128)}, u32[]{:S(2)}) copy-start(s32[16]{0:T(128)} %param.14) | copy-start | bytes 196
  7.2 14.2 %copy-start.1 = (bf16[256,512]{1,0:T(8,128)(2,1)S(1)}, bf16[256,512]{1,0:T(8,128)(2,1)}, u32[]{:S(2)}) copy-start(bf16[256,512]{1,0:T(8,128)(2,1)} %param.13) | copy-start | bytes 786436
  7.2 49.5 %all-gather.3.cloned.1.call-start = ((), (), s32[]{:S(2)}) async-start(), calls=%async_computation.3 | async-start | bytes 2162688 | tf_op jit(solution)/shard_map/all_gather | solution.py:130
  7.9 94.0 %all-gather.5.cloned.1.call-start = ((), (), s32[]{:S(2)}) async-start(), calls=%async_computation.4 | async-start | bytes 2162688 | tf_op jit(solution)/shard_map/all_gather | solution.py:131
  12.2 17.5 %all-to-all-start = ((bf16[32,8,512]{2,1,0:T(8,128)(2,1)}), bf16[32,8,512]{2,1,0:T(8,128)(2,1)S(1)}, u32[]{:S(2)}, u32[]{:S(2)}) async-start(bf16[32,8,512]{2,1,0:T(8,128)(2,1)} %bitcast_select_fusion.2), calls=%async_computation | async-start | bytes 524288 | tf_op jit(solution)/shard_map/all_to_all | solution.py:115
  20.7 382.6 %reduce-scatter.5.cloned.1.call-start = ((), (), s32[]{:S(2)}) async-start(), calls=%async_computation.6 | async-start | bytes 4325376 | tf_op jit(solution)/shard_map/reduce_scatter | solution.py:158
  20.8 81.2 %copy-start.2 = (s32[32,8]{1,0:T(8,128)}, s32[32,8]{1,0:T(8,128)S(1)}, u32[]{:S(2)}) copy-start(s32[32,8]{1,0:T(8,128)S(1)} %dynamic-slice_add_fusion) | copy-start | bytes 3076
  321.4 167.7 %reduce-scatter.3.cloned.1.call-start = ((), (), s32[]{:S(2)}) async-start(), calls=%async_computation.5 | async-start | bytes 4325376 | tf_op jit(solution)/shard_map/reduce_scatter | solution.py:157
Sparse Core Ops, SparseCore 0:
  10.3 46.3 all-gather.2
  59.0 42.9 all-gather.4
  321.5 81.6 reduce-scatter.4
  407.3 81.6 reduce-scatter.2
where the time goes:
time: 498 us; the launch traced here: 496 us
  waiting for transfers between devices  247 us (50%)
  matrix products  160 us (32%)
  other arithmetic  41.9 us (8%)
  local copies, waits for them, and re-layouts  22.7 us (5%)
  between operations  14 us (3%)
  starting transfers between devices  8.6 us (2%)
    reduce_scatter x1, waiting for transfers between devices, per_device(): lax.psum_scatter(key_all, 'seq', scatter_dimension=0, tiled=True)  85.8 us
    reduce_scatter x1, waiting for transfers between devices, per_device(): lax.psum_scatter(value_all, 'seq', scatter_dimension=0, tiled=True)  79.4 us
    dot_general x32, matrix products, block_scores(): jnp.einsum('bhd,td->bht', query_heads, key_block, preferred_element_type=...  47.9 us
    all_gather x1, waiting for transfers between devices, per_device(): lax.all_gather(values, 'seq', axis=0, tiled=True)  45.3 us
    dot_general x16, matrix products, forward_update(): jnp.einsum('bht,td->bhd', exp_weights.astype(jnp.bfloat16), value_block,...  28.7 us
    all_gather x1, waiting for transfers between devices, per_device(): lax.all_gather(keys, 'seq', axis=0, tiled=True)  26.8 us
    dot_general x16, matrix products, backward_update(): jnp.einsum('bht,td->bhd', score_grads, key_block, preferred_element_type=...  24.8 us
    dot_general x16, matrix products, backward_update(): jnp.einsum('bhd,td->bht', grad_heads, value_block, preferred_element_type...  21.5 us
  transfers between devices with their start and end apart: 5, of which 5 were waited for; matrix products, arithmetic and copies ran while one was open for 1% of the time, Pallas kernels for 0%

commit v1 on v0

--- a/solution.py
+++ b/solution.py
@@ -128,7 +128,9 @@
     )
     piece_pair = (
         lax.all_gather(keys, "seq", axis=0, tiled=True),
-        lax.all_gather(values, "seq", axis=0, tiled=True),
+        jnp.concatenate(
+            lax.all_to_all(jnp.stack([values] * lax.axis_size("seq")), "seq", 0, 0), axis=0
+        ),
     )
     run_max, run_total, weighted = forward_piece(start_state, piece_pair[0], piece_pair[1], context)
     attended = weighted / run_total[:, :, None]

time: 498 us -> 463 us (0.930)
  waiting for transfers between devices: 247 us -> 198 us
  blocking collectives: 0 us -> 17.2 us
    all_gather x1, waiting for transfers between devices: 45.3 us -> 0.02 us  [per_device(): lax.all_gather(values, 'seq', axis=0, tiled=True)]
    all_gather x1, waiting for transfers between devices: 26.8 us -> 2.88 us  [per_device(): lax.all_gather(keys, 'seq', axis=0, tiled=True)]
    all_to_all x1, waiting for transfers between devices: 7.96 us -> 28.7 us  [per_device(): lax.all_to_all(jnp.stack([values] * lax.axis_size('seq')), 'seq', 0, 0)]
    all_to_all x0 -> x1, blocking collectives: none -> 17.2 us  [per_device(): lax.all_to_all(outgoing, 'seq', split_axis=0, concat_axis=0, tiled=True)]
  transfers between devices with their start and end apart: 5 -> 5, of which waited for: 5 -> 4; matrix products, arithmetic and copies ran while one was open for 1% -> 20% of each run, Pallas kernels for 0% -> 0%
where the time goes in v1:
time: 463 us; the launch traced here: 461 us
  waiting for transfers between devices  198 us (43%)
  matrix products  160 us (35%)
  other arithmetic  41.2 us (9%)
  local copies, waits for them, and re-layouts  24.5 us (5%)
  blocking collectives  17.2 us (4%)
  between operations  14 us (3%)
  starting transfers between devices  5.05 us (1%)
    reduce_scatter x1, waiting for transfers between devices, per_device(): lax.psum_scatter(key_all, 'seq', scatter_dimension=0, tiled=True)  85.8 us
    reduce_scatter x1, waiting for transfers between devices, per_device(): lax.psum_scatter(value_all, 'seq', scatter_dimension=0, tiled=True)  78.8 us
    dot_general x32, matrix products, block_scores(): jnp.einsum('bhd,td->bht', query_heads, key_block, preferred_element_type=...  47.9 us
    dot_general x16, matrix products, forward_update(): jnp.einsum('bht,td->bhd', exp_weights.astype(jnp.bfloat16), value_block,...  28.7 us
    all_to_all x1, waiting for transfers between devices, per_device(): lax.all_to_all(jnp.stack([values] * lax.axis_size('seq')), 'seq', 0, 0)  28.7 us
    dot_general x16, matrix products, backward_update(): jnp.einsum('bht,td->bhd', score_grads, key_block, preferred_element_type=...  24.9 us
    dot_general x16, matrix products, backward_update(): jnp.einsum('bhd,td->bht', grad_heads, value_block, preferred_element_type...  21.5 us
    dynamic_slice x32, local copies, waits for them, and re-layouts, forward_piece(): run_state, _ = lax.scan(forward_update, run_state, stacked)  18.7 us
  transfers between devices with their start and end apart: 5, of which 4 were waited for; matrix products, arithmetic and copies ran while one was open for 20% of the time, Pallas kernels for 0%

profile of v1, /device:TPU:0, one launch (start us, length us, event | category | flops | bytes accessed | tf_op | source)
XLA Modules:
  0.0 461.3 jit_solution(13468308851842516548)
XLA Ops:
  10.7 17.2 %all_to_all.11 = bf16[32,8,512]{2,1,0:T(8,128)(2,1)S(1)} all-to-all(bf16[32,8,512]{2,1,0:T(8,128)(2,1)S(1)} %bitcast_select_fusion.2), channel_id=1, replica_groups=mesh['seq'=32,'head'=4] {'seq'}, dimensions={0} | all-to-all | bytes 524288 | tf_op jit(solution)/shard_map/all_to_all | solution.py:115
  27.9 1.8 stack.2
  29.7 4.9 %all-to-all-start.1 = ((bf16[32,256,128]{2,1,0:T(8,128)(2,1)}), bf16[32,256,128]{2,1,0:T(8,128)(2,1)}, u32[]{:S(2)}, u32[]{:S(2)}) async-start(bf16[32,256,128]{2,1,0:T(8,128)(2,1)} %stack.2), calls=%async_computation.1 | async-start | bytes 4194304 | tf_op jit(solution)/shard_map/all_to_all | solution.py:132
  36.6 28.7 %all-to-all-done.1 = bf16[32,256,128]{2,1,0:T(8,128)(2,1)} async-done(((bf16[32,256,128]{2,1,0:T(8,128)(2,1)}), bf16[32,256,128]{2,1,0:T(8,128)(2,1)}, u32[]{:S(2)}, u32[]{:S(2)}) %all-to-all-start.1) | async-done | bytes 2097184 | tf_op jit(solution)/shard_map/all_to_all | solution.py:132
  65.3 2.9 all-gather.3.cloned.1.call-done
  68.2 85.3 %while.32 = (s32[]{:T(128)}, f32[256,4]{0,1:T(4,128)S(1)}, f32[256,4]{0,1:T(4,128)S(1)}, f32[256,4,128]{2,0,1:T(8,128)S(1)}, s32[256]{0:T(256)S(1)}, /*index=5*/...) while((s32[]{:T(128)}, f32[256,4]{0,1:T(4,128)S(1)}, ...), condition=%wide.wide.region_6.7_spmd.clone, body=%wide.wide.region_2.6_spmd.clone.sunk | while | flops 276067328 | bytes 8466673 | solution.py:65
  69.8 1.4 fusion.88
  71.7 1.8 convolution_add_fusion.6
  75.1 1.4 fusion.88
  77.1 1.8 convolution_add_fusion.6
  80.4 1.4 fusion.88
  82.4 1.8 convolution_add_fusion.6
  87.7 1.8 convolution_add_fusion.6
  91.1 1.4 fusion.88
  93.0 1.8 convolution_add_fusion.6
  96.4 1.4 fusion.88
  98.4 1.8 convolution_add_fusion.6
  101.7 1.4 fusion.88
  103.7 1.8 convolution_add_fusion.6
  107.1 1.4 fusion.88
  109.1 1.8 convolution_add_fusion.6
  114.4 1.8 convolution_add_fusion.6
  119.7 1.8 convolution_add_fusion.6
  125.0 1.8 convolution_add_fusion.6
  130.4 1.8 convolution_add_fusion.6
  135.7 1.8 convolution_add_fusion.6
  141.0 1.8 convolution_add_fusion.6
  146.4 1.8 convolution_add_fusion.6
  151.7 1.8 convolution_add_fusion.6
  153.9 133.8 %while.33 = (s32[]{:T(128)}, f32[256,4,128]{2,0,1:T(8,128)S(1)}, f32[16,512,128]{2,1,0:T(8,128)}, f32[16,512,128]{2,1,0:T(8,128)}, s32[256]{0:T(256)S(1)}, /*ind...) while((s32[]{:T(128)}, f32[256,4,128]{2,0,1:T(8,128)S(1)}, ...), condition=%wide.wide.region_10.11_spmd.clone, body=%wide.wide.region_8.10_spmd.clone.sunk | while | flops 676028416 | bytes 12734739 | solution.py:100
  155.4 1.6 fusion.101
  158.4 1.6 convolution_add_fusion.7
  163.7 1.6 fusion.101
  166.7 1.6 convolution_add_fusion.7
  172.1 1.6 fusion.101
  175.0 1.6 convolution_add_fusion.7
  180.4 1.6 fusion.101
  183.4 1.6 convolution_add_fusion.7
  188.8 1.6 fusion.101
  191.8 1.6 convolution_add_fusion.7
  197.2 1.6 fusion.101
  200.2 1.6 convolution_add_fusion.7
  205.6 1.6 fusion.101
  208.5 1.6 convolution_add_fusion.7
  213.9 1.6 fusion.101
  216.9 1.6 convolution_add_fusion.7
  222.3 1.6 fusion.101
  225.3 1.6 convolution_add_fusion.7
  230.7 1.6 fusion.101
  233.6 1.6 convolution_add_fusion.7
  239.0 1.6 fusion.101
  242.0 1.6 convolution_add_fusion.7
  247.4 1.6 fusion.101
  250.4 1.6 convolution_add_fusion.7
  255.8 1.6 fusion.101
  258.7 1.6 convolution_add_fusion.7
  264.1 1.6 fusion.101
  267.1 1.6 convolution_add_fusion.7
  272.5 1.6 fusion.101
  275.4 1.6 convolution_add_fusion.7
  280.8 1.6 fusion.101
  283.8 1.6 convolution_add_fusion.7
  290.1 78.8 %reduce-scatter.5.cloned.1.call-done = f32[256,128]{1,0:T(8,128)} async-done(((f32[8192,128]{1,0:T(8,128)}), f32[256,128]{1,0:T(8,128)}) %reduce-scatter.5.cloned.1.call-update) | async-done | bytes 131088 | tf_op jit(solution)/shard_map/reduce_scatter | solution.py:160
  368.9 85.8 %reduce-scatter.3.cloned.1.call-done = f32[256,128]{1,0:T(8,128)} async-done(((f32[8192,128]{1,0:T(8,128)}), f32[256,128]{1,0:T(8,128)}) %reduce-scatter.3.cloned.1.call-update) | async-done | bytes 131088 | tf_op jit(solution)/shard_map/reduce_scatter | solution.py:159
  (302 shorter events, 136.7 us)
Async XLA Ops:
  7.2 2.3 copy-start
  7.2 20.7 %copy-start.1 = (bf16[256,128]{1,0:T(8,128)(2,1)S(1)}, bf16[256,128]{1,0:T(8,128)(2,1)}, u32[]{:S(2)}) copy-start(bf16[256,128]{1,0:T(8,128)(2,1)} %param.12) | copy-start | bytes 196612
  7.2 61.0 %all-gather.3.cloned.1.call-start = ((), (), s32[]{:S(2)}) async-start(), calls=%async_computation.4 | async-start | bytes 2162688 | tf_op jit(solution)/shard_map/all_gather | solution.py:130
  29.7 5.7 %copy-start.4 = (s32[32,256]{1,0:T(8,128)S(1)}, s32[32,256]{1,0:T(8,128)}, u32[]{:S(2)}) copy-start(s32[32,256]{1,0:T(8,128)} %param.15) | copy-start | bytes 98308
  29.7 6.1 %copy-start.5 = (s32[16]{0:T(128)S(1)}, s32[16]{0:T(128)}, u32[]{:S(2)}) copy-start(s32[16]{0:T(128)} %param.14) | copy-start | bytes 196
  29.7 6.4 %copy-start.2 = (bf16[256,512]{1,0:T(8,128)(2,1)S(1)}, bf16[256,512]{1,0:T(8,128)(2,1)}, u32[]{:S(2)}) copy-start(bf16[256,512]{1,0:T(8,128)(2,1)} %param.13) | copy-start | bytes 786436
  29.7 35.6 %all-to-all-start.1 = ((bf16[32,256,128]{2,1,0:T(8,128)(2,1)}), bf16[32,256,128]{2,1,0:T(8,128)(2,1)}, u32[]{:S(2)}, u32[]{:S(2)}) async-start(bf16[32,256,128]{2,1,0:T(8,128)(2,1)} %stack.2), calls=%async_computation.1 | async-start | bytes 4194304 | tf_op jit(solution)/shard_map/all_to_all | solution.py:132
  34.6 119.2 %all-gather.5.cloned.1.call-start = ((), (), s32[]{:S(2)}) async-start(), calls=%async_computation.5 | async-start | bytes 2162688 | tf_op jit(solution)/shard_map/all_gather | solution.py:152
  35.4 333.6 %reduce-scatter.5.cloned.1.call-start = ((), (), s32[]{:S(2)}) async-start(), calls=%async_computation.7 | async-start | bytes 4325376 | tf_op jit(solution)/shard_map/reduce_scatter | solution.py:160
  35.5 32.7 %copy-start.3 = (s32[32,8]{1,0:T(8,128)}, s32[32,8]{1,0:T(8,128)S(1)}, u32[]{:S(2)}) copy-start(s32[32,8]{1,0:T(8,128)S(1)} %dynamic-slice_add_fusion) | copy-start | bytes 3076
  287.7 167.1 %reduce-scatter.3.cloned.1.call-start = ((), (), s32[]{:S(2)}) async-start(), calls=%async_computation.6 | async-start | bytes 4325376 | tf_op jit(solution)/shard_map/reduce_scatter | solution.py:159
Sparse Core Ops, SparseCore 0:
  10.3 57.9 all-gather.2
  70.5 42.3 all-gather.4
  287.8 81.0 reduce-scatter.4
  373.0 81.7 reduce-scatter.2
